TPU v7x, 512 devices: a whole 4x4x16 slice. The times are simulated.
512 devices in a mesh: pipe: 4 (over y), expert: 32 (over z, core), tensor: 4 (over x).
Axes of the slice: x: 4, y: 4, z: 16, core: 2. Of those that a mesh axis runs over, the one named last changes fastest.
Arguments:
- tokens: bfloat16 [512, 6144], P('expert', ('pipe', 'tensor')), may hold values from -6 to 6
- expert_ids: int32 [512, 2], P('expert'), may hold values from 0 to 7, all different within a row; in each aligned block of 16 rows (0 to 15, 16 to 31, ...) at most 5 rows name the same one
- gates: float32 [512, 2], P('expert'), may hold values from 0.2 to 1
- w_gate: bfloat16 [32, 6144, 2048], P('expert', None, ('pipe', 'tensor')), may hold values from -0.078125 to 0.078125
- w_up: bfloat16 [32, 6144, 2048], P('expert', None, ('pipe', 'tensor')), may hold values from -0.078125 to 0.078125
- w_down: bfloat16 [32, 2048, 6144], P('expert', ('pipe', 'tensor')), may hold values from -0.0625 to 0.0625
- d_out: bfloat16 [512, 6144], P('expert', ('pipe', 'tensor')), may hold values from -6 to 6
Outputs:
- moe_out: bfloat16 [512, 6144], P('expert', ('pipe', 'tensor'))
- grad_tokens: bfloat16 [512, 6144], P('expert', ('pipe', 'tensor'))
- grad_gates: float32 [512, 2], P('expert')
Inputs may be any that keep to these rules, and one draw needn't show every extreme that they name: `expert_ids`: each row names 2 different experts. Among the rows of one index of expert (aligned blocks of 16 rows) no expert is named more than 5 times, a bound that some block reaches.
All inputs are finite; a program needn't handle non-finite values.
Results may differ from a plain program's by a relative error of at most 0.017.
Values may be sent and summed in bfloat16 or wider, within the bound.
No kernel may reach another device: no remote copies, remote signals or barrier semaphores. Data moves between devices by JAX's collectives and lax.ppermute only.
A program may use at most 64 MiB of HBM per device.

v0:
```python
import jax
import jax.numpy as jnp
from jax import lax
from jax.sharding import PartitionSpec as P


def per_device(tokens, expert_ids, gates, w_gate, w_up, w_down, d_out):
    tok_rows = tokens.shape[0]
    feat = tokens.shape[1]
    top = expert_ids.shape[1]
    devices_all = lax.axis_size("expert")
    experts = min(8, devices_all)
    group = devices_all // experts
    capacity = min(
        tok_rows,
        max(2, max(5 * tok_rows * top // (4 * experts), (tok_rows * top + experts - 1) // experts)),
    )
    slots = experts * capacity
    flat_ids = expert_ids.reshape(-1)
    onehot = (flat_ids[:, None] == jnp.arange(experts, dtype=jnp.int32)[None, :]).astype(jnp.int32)
    position = jnp.sum(jnp.cumsum(onehot, axis=0) * onehot, axis=1) - 1
    slot_of = flat_ids * capacity + position
    picks = (jnp.arange(slots, dtype=jnp.int32)[:, None] == slot_of[None, :]).astype(jnp.float32)
    pick_rows = picks.reshape(slots, tok_rows, top)
    select_tok = jnp.sum(pick_rows, axis=2).astype(jnp.bfloat16)
    select_gate = jnp.sum(pick_rows * gates[None, :, :], axis=2)
    picked = jnp.dot(select_tok, tokens, preferred_element_type=jnp.float32).astype(jnp.bfloat16)
    scaled = jnp.dot(
        select_gate, d_out.astype(jnp.float32), precision=lax.Precision.HIGHEST
    ).astype(jnp.bfloat16)
    send = jnp.concatenate([picked, scaled], axis=1).reshape(experts, capacity, 2 * feat)
    send = jnp.repeat(send, group, axis=0)
    recv = lax.all_to_all(send, "expert", split_axis=0, concat_axis=0, tiled=True)
    recv = recv.reshape(devices_all * capacity, 2 * feat)
    part_x = recv[:, :feat]
    part_dy = recv[:, feat:]
    rows_x = lax.all_gather(part_x, ("pipe", "tensor"), axis=1, tiled=True)
    rows_dy = lax.all_gather(part_dy, ("pipe", "tensor"), axis=1, tiled=True)
    gate_proj = w_gate[0]
    up_proj = w_up[0]
    down_proj = w_down[0]
    contract_last = (((1,), (1,)), ((), ()))
    h_gate = jnp.dot(rows_x, gate_proj, preferred_element_type=jnp.float32)
    h_up = jnp.dot(rows_x, up_proj, preferred_element_type=jnp.float32)
    sig = jax.nn.sigmoid(h_gate)
    hidden = (h_gate * sig * h_up).astype(jnp.bfloat16)
    out_terms = jnp.dot(hidden, down_proj, preferred_element_type=jnp.float32)
    d_hidden = lax.dot_general(
        rows_dy, down_proj, contract_last, preferred_element_type=jnp.float32
    )
    d_gate_h = (d_hidden * h_up * sig * (1.0 + h_gate * (1.0 - sig))).astype(jnp.bfloat16)
    d_up_h = (d_hidden * h_gate * sig).astype(jnp.bfloat16)
    dx_terms = lax.dot_general(
        d_gate_h, gate_proj, contract_last, preferred_element_type=jnp.float32
    )
    dx_terms = dx_terms + lax.dot_general(
        d_up_h, up_proj, contract_last, preferred_element_type=jnp.float32
    )
    out_share = lax.psum_scatter(
        out_terms.astype(jnp.bfloat16), ("pipe", "tensor"), scatter_dimension=1, tiled=True
    )
    dx_share = lax.psum_scatter(
        dx_terms.astype(jnp.bfloat16), ("pipe", "tensor"), scatter_dimension=1, tiled=True
    )
    back_send = jnp.concatenate([out_share, dx_share], axis=1).reshape(
        devices_all, capacity, 2 * feat
    )
    back = lax.all_to_all(back_send, "expert", split_axis=0, concat_axis=0, tiled=True)
    back_rows = (
        jnp.sum(back.astype(jnp.float32).reshape(experts, group, capacity, 2 * feat), axis=1)
        .astype(jnp.bfloat16)
        .reshape(slots, 2 * feat)
    )
    assign = picks.T.astype(jnp.bfloat16)
    a_both = jnp.dot(assign, back_rows, preferred_element_type=jnp.float32)
    a_out = a_both[:, :feat].reshape(tok_rows, top, feat)
    a_dx = a_both[:, feat:].reshape(tok_rows, top, feat)
    moe_out = jnp.sum(gates[:, :, None] * a_out, axis=1).astype(jnp.bfloat16)
    grad_tokens = jnp.sum(a_dx, axis=1).astype(jnp.bfloat16)
    partial_dots = jnp.sum(d_out.astype(jnp.float32)[:, None, :] * a_out, axis=2)
    grad_gates = lax.psum(partial_dots, ("pipe", "tensor"))
    return (moe_out, grad_tokens, grad_gates)


def solution(mesh):
    return jax.shard_map(
        per_device,
        mesh=mesh,
        in_specs=(
            P("expert", ("pipe", "tensor")),
            P("expert", None),
            P("expert", None),
            P("expert", None, ("pipe", "tensor")),
            P("expert", None, ("pipe", "tensor")),
            P("expert", ("pipe", "tensor"), None),
            P("expert", ("pipe", "tensor")),
        ),
        out_specs=(
            P("expert", ("pipe", "tensor")),
            P("expert", ("pipe", "tensor")),
            P("expert", None),
        ),
        check_vma=False,
    )
```

profile of v0, /device:TPU:32, one launch (start us, length us, event | category | flops | bytes accessed | tf_op | source)
XLA Modules:
  0.0 457.4 jit_solution(14242704866884179317)
XLA Ops:
  7.2 0.9 copy.35
  9.4 0.8 convert_reduce_fusion
  10.1 0.9 convolution_convert_fusion.1
  11.1 0.9 convolution_convert_fusion.2
  12.1 41.8 %all_to_all.10 = bf16[32,5,768]{2,1,0:T(8,128)(2,1)S(1)} all-to-all(bf16[32,5,768]{2,1,0:T(8,128)(2,1)S(1)} %bitcast.32), channel_id=1, replica_groups=mesh['pipe'=4,'expert'=32,'tensor'=4] {'expert'}, dimensions={0} | all-to-all | bytes 491520 | tf_op jit(solution)/shard_map/all_to_all | solution.py:33
  54.0 0.7 fusion.21
  55.6 54.5 %all-gather.3.cloned.1.call-done = bf16[160,6144]{1,0:T(8,128)(2,1)} async-done(((bf16[160,384]{1,0:T(8,128)(2,1)}), bf16[160,6144]{1,0:T(8,128)(2,1)}) %all-gather.3.cloned.1.call-update) | async-done | bytes 1966096 | tf_op jit(solution)/shard_map/all_gather | solution.py:37
  110.0 2.3 fusion.9
  112.4 2.2 fusion.5
  114.6 60.3 %all-gather.5.cloned.1.call-done = bf16[160,6144]{1,0:T(8,128)(2,1)} async-done(((bf16[160,384]{1,0:T(8,128)(2,1)}), bf16[160,6144]{1,0:T(8,128)(2,1)}) %all-gather.5.cloned.1.call-update) | async-done | bytes 1966096 | tf_op jit(solution)/shard_map/all_gather | solution.py:38
  174.9 2.2 fusion.1
  178.5 1.6 fusion
  180.1 2.8 copy.40
  182.9 2.2 convolution_convert_fusion
  185.1 2.8 copy.38
  187.9 85.6 %reduce-scatter.9.cloned.1.call-done = bf16[384,160]{1,0:T(8,128)(2,1)} async-done(((bf16[6144,160]{1,0:T(8,128)(2,1)}), bf16[384,160]{1,0:T(8,128)(2,1)}) %reduce-scatter.9.cloned.1.call-update) | async-done | bytes 122896
  273.6 1.1 copy.41
  274.6 93.5 %reduce-scatter.7.cloned.1.call-done = bf16[384,160]{1,0:T(8,128)(2,1)} async-done(((bf16[6144,160]{1,0:T(8,128)(2,1)}), bf16[384,160]{1,0:T(8,128)(2,1)}) %reduce-scatter.7.cloned.1.call-update) | async-done | bytes 122896
  368.1 1.1 copy.39
  369.2 0.8 reshape.67
  370.1 12.8 %all-to-all-start.1 = ((bf16[32,5,768]{2,1,0:T(8,128)(2,1)}), bf16[32,5,768]{2,1,0:T(8,128)(2,1)S(1)}, u32[]{:S(2)}, u32[]{:S(2)}) async-start(bf16[32,5,768]{2,1,0:T(8,128)(2,1)} %reshape.67), calls=%async_computation.1 | async-start | bytes 786432 | tf_op jit(solution)/shard_map/all_to_all | solution.py:68
  383.0 26.5 %all-to-all-done.1 = bf16[32,5,768]{2,1,0:T(8,128)(2,1)S(1)} async-done(((bf16[32,5,768]{2,1,0:T(8,128)(2,1)}), bf16[32,5,768]{2,1,0:T(8,128)(2,1)S(1)}, u32[]{:S(2)}, u32[]{:S(2)}) %all-to-all-start.1) | async-done | bytes 245792 | tf_op jit(solution)/shard_map/all_to_all | solution.py:68
  410.2 38.6 %psum.7 = f32[16,2]{1,0:T(8,128)S(1)} all-reduce(f32[16,2]{1,0:T(8,128)S(1)} %reduce_sum.72), channel_id=1, replica_groups=mesh['pipe'=4,'expert'=32,'tensor'=4] {'pipe','tensor'}, use_global_device_ids=true, to_apply=%region_10.11 | all-reduce | flops 32 | bytes 256 | tf_op jit(solution)/shard_map/psum | solution.py:81
  449.5 0.7 multiply_reduce_fusion.1
  (50 shorter events, 5.8 us)
Async XLA Ops:
  7.2 102.9 %copy-start = (bf16[1,6144,128]{2,1,0:T(8,128)(2,1)S(1)}, bf16[1,6144,128]{2,1,0:T(8,128)(2,1)}, u32[]{:S(2)}) copy-start(bf16[1,6144,128]{2,1,0:T(8,128)(2,1)} %param.10) | copy-start | bytes 4718596
  7.2 102.8 %all-gather.3.cloned.1.call-start = ((), (), s32[]{:S(2)}) async-start(), calls=%async_computation.4 | async-start | bytes 2088960 | tf_op jit(solution)/shard_map/all_gather | solution.py:37
  54.8 120.1 %all-gather.5.cloned.1.call-start = ((), (), s32[]{:S(2)}) async-start(), calls=%async_computation.5 | async-start | bytes 2088960 | tf_op jit(solution)/shard_map/all_gather | solution.py:38
  55.5 218.1 %reduce-scatter.9.cloned.1.call-start = ((), (), s32[]{:S(2)}) async-start(), calls=%async_computation.7 | async-start | bytes 3342336
  110.0 2.4 copy-start.1
  112.4 64.7 %copy-start.4 = (f32[160,128]{1,0:T(8,128)}, f32[160,128]{1,0:T(8,128)S(1)}, u32[]{:S(2)}) copy-start(f32[160,128]{1,0:T(8,128)S(1)} %fusion.9) | copy-start | bytes 245764
  112.4 62.5 %copy-start.2 = (bf16[1,128,6144]{2,1,0:T(8,128)(2,1)S(1)}, bf16[1,128,6144]{2,1,0:T(8,128)(2,1)}, u32[]{:S(2)}) copy-start(bf16[1,128,6144]{2,1,0:T(8,128)(2,1)} %param.12) | copy-start | bytes 4718596
  114.6 62.5 %copy-start.5 = (f32[160,128]{1,0:T(8,128)}, f32[160,128]{1,0:T(8,128)S(1)}, u32[]{:S(2)}) copy-start(f32[160,128]{1,0:T(8,128)S(1)} %fusion.5) | copy-start | bytes 245764
  177.1 1.4 copy-start.3
  182.9 185.2 %reduce-scatter.7.cloned.1.call-start = ((), (), s32[]{:S(2)}) async-start(), calls=%async_computation.6 | async-start | bytes 3342336
  187.9 195.0 %copy-start.7 = (f32[16,2]{0,1:T(2,128)S(1)}, f32[16,2]{0,1:T(2,128)}, u32[]{:S(2)}) copy-start(f32[16,2]{0,1:T(2,128)} %param.9) | copy-start | bytes 388
  187.9 195.1 %copy-start.6 = (bf16[16,384]{1,0:T(8,128)(2,1)S(1)}, bf16[16,384]{1,0:T(8,128)(2,1)}, u32[]{:S(2)}) copy-start(bf16[16,384]{1,0:T(8,128)(2,1)} %param.13) | copy-start | bytes 36868
  370.1 39.5 %all-to-all-start.1 = ((bf16[32,5,768]{2,1,0:T(8,128)(2,1)}), bf16[32,5,768]{2,1,0:T(8,128)(2,1)S(1)}, u32[]{:S(2)}, u32[]{:S(2)}) async-start(bf16[32,5,768]{2,1,0:T(8,128)(2,1)} %reshape.67), calls=%async_computation.1 | async-start | bytes 786432 | tf_op jit(solution)/shard_map/all_to_all | solution.py:68
Sparse Core Ops, SparseCore 0:
  54.9 55.0 all-gather.2
  113.0 61.8 all-gather.4
  183.0 90.5 reduce-scatter.8
  277.6 90.4 reduce-scatter.6
where the time goes:
time: 458 us; the launch traced here: 457 us
  waiting for transfers between devices  321 us (70%)
  blocking collectives  80.5 us (18%)
  between operations  14 us (3%)
  matrix products  13.2 us (3%)
  starting transfers between devices  13 us (3%)
  local copies, waits for them, and re-layouts  12.2 us (3%)
    unnamed x6, waiting for transfers between devices  180 us
    all_gather x1, waiting for transfers between devices, per_device(): rows_dy = lax.all_gather(part_dy, ('pipe', 'tensor'), axis=1, tiled=True)  60.3 us
    all_gather x1, waiting for transfers between devices, per_device(): rows_x = lax.all_gather(part_x, ('pipe', 'tensor'), axis=1, tiled=True)  54.5 us
    all_to_all x1, blocking collectives, per_device(): lax.all_to_all(send, 'expert', split_axis=0, concat_axis=0, tiled=True)  41.8 us
    psum x1, blocking collectives, per_device(): grad_gates = lax.psum(partial_dots, ('pipe', 'tensor'))  38.6 us
    all_to_all x1, waiting for transfers between devices, per_device(): lax.all_to_all(back_send, 'expert', split_axis=0, concat_axis=0, tiled=True)  26.5 us
    all_to_all x1, starting transfers between devices, per_device(): lax.all_to_all(back_send, 'expert', split_axis=0, concat_axis=0, tiled=True)  12.8 us
    unnamed x23, local copies, waits for them, and re-layouts  9.97 us
  transfers between devices with their start and end apart: 5, of which 5 were waited for; matrix products, arithmetic and copies ran while one was open for 2% of the time, Pallas kernels for 0%

commit v1 on v0

--- a/solution.py
+++ b/solution.py
@@ -2,6 +2,24 @@
 import jax.numpy as jnp
 from jax import lax
 from jax.sharding import PartitionSpec as P
+
+
+def collect(value, axis, dim):
+    ways, here, step = (lax.axis_size(axis), lax.axis_index(axis), value.shape[dim])
+    shape = [n * ways if d == dim else n for d, n in enumerate(value.shape)]
+    full = lax.dynamic_update_slice_in_dim(
+        jnp.zeros(shape, value.dtype), value, here * step, axis=dim
+    )
+    going_up = going_down = value
+    for far in range(1, ways // 2 + 1):
+        going_up = lax.ppermute(going_up, axis, [(d, (d + 1) % ways) for d in range(ways)])
+        full = lax.dynamic_update_slice_in_dim(full, going_up, (here - far) % ways * step, axis=dim)
+        if 2 * far < ways:
+            going_down = lax.ppermute(going_down, axis, [(d, (d - 1) % ways) for d in range(ways)])
+            full = lax.dynamic_update_slice_in_dim(
+                full, going_down, (here + far) % ways * step, axis=dim
+            )
+    return full
 
 
 def per_device(tokens, expert_ids, gates, w_gate, w_up, w_down, d_out):
@@ -34,7 +52,7 @@
     recv = recv.reshape(devices_all * capacity, 2 * feat)
     part_x = recv[:, :feat]
     part_dy = recv[:, feat:]
-    rows_x = lax.all_gather(part_x, ("pipe", "tensor"), axis=1, tiled=True)
+    rows_x = collect(part_x, ("pipe", "tensor"), 1)
     rows_dy = lax.all_gather(part_dy, ("pipe", "tensor"), axis=1, tiled=True)
     gate_proj = w_gate[0]
     up_proj = w_up[0]

time: 458 us -> 414 us (0.904)
  waiting for transfers between devices: 321 us -> 235 us
  starting transfers between devices: 13 us -> 95.7 us
  blocking collectives: 80.5 us -> 38.7 us
  matrix products: 13.2 us -> 7.68 us
  local copies, waits for them, and re-layouts: 12.2 us -> 17.4 us
    ppermute x0 -> x15, starting transfers between devices: none -> 67.4 us  [the longest x7 50.6 us: collect(): lax.ppermute(going_down, axis, [(d, (d - 1) % ways) for d in range(ways)])]
    all_gather x1, waiting for transfers between devices: 60.3 us -> 0.02 us  [per_device(): rows_dy = lax.all_gather(part_dy, ('pipe', 'tensor'), axis=1, tiled=True)]
    all_gather x1 -> x0, waiting for transfers between devices: 54.5 us -> none  [per_device(): rows_x = lax.all_gather(part_x, ('pipe', 'tensor'), axis=1, tiled=True)]
    all_to_all x1 -> x0, blocking collectives: 41.8 us -> none  [per_device(): lax.all_to_all(send, 'expert', split_axis=0, concat_axis=0, tiled=True)]
    all_to_all x0 -> x1, waiting for transfers between devices: none -> 26.6 us  [per_device(): lax.all_to_all(send, 'expert', split_axis=0, concat_axis=0, tiled=True)]
    all_to_all x0 -> x1, starting transfers between devices: none -> 15.3 us  [per_device(): lax.all_to_all(send, 'expert', split_axis=0, concat_axis=0, tiled=True)]
    ppermute x0 -> x15, waiting for transfers between devices: none -> 13.4 us  [the longest x8 12.5 us: collect(): lax.ppermute(going_up, axis, [(d, (d + 1) % ways) for d in range(ways)])]
    unnamed x6 -> x5, waiting for transfers between devices: 180 us -> 169 us
  transfers between devices with their start and end apart: 5 -> 20, of which waited for: 5 -> 15; matrix products, arithmetic and copies ran while one was open for 2% -> 4% of each run, Pallas kernels for 0% -> 0%
where the time goes in v1:
time: 414 us; the launch traced here: 413 us
  waiting for transfers between devices  235 us (57%)
  starting transfers between devices  95.7 us (23%)
  blocking collectives  38.7 us (9%)
  local copies, waits for them, and re-layouts  17.4 us (4%)
  between operations  14.6 us (4%)
  matrix products  7.68 us (2%)
    unnamed x5, waiting for transfers between devices  169 us
    ppermute x7, starting transfers between devices, collect(): lax.ppermute(going_down, axis, [(d, (d - 1) % ways) for d in range(ways)])  50.6 us
    psum x1, blocking collectives, per_device(): grad_gates = lax.psum(partial_dots, ('pipe', 'tensor'))  38.7 us
    all_to_all x1, waiting for transfers between devices, per_device(): lax.all_to_all(send, 'expert', split_axis=0, concat_axis=0, tiled=True)  26.6 us
    all_to_all x1, waiting for transfers between devices, per_device(): lax.all_to_all(back_send, 'expert', split_axis=0, concat_axis=0, tiled=True)  26.5 us
    ppermute x8, starting transfers between devices, collect(): lax.ppermute(going_up, axis, [(d, (d + 1) % ways) for d in range(ways)])  16.8 us
    all_to_all x1, starting transfers between devices, per_device(): lax.all_to_all(send, 'expert', split_axis=0, concat_axis=0, tiled=True)  15.3 us
    all_to_all x1, starting transfers between devices, per_device(): lax.all_to_all(back_send, 'expert', split_axis=0, concat_axis=0, tiled=True)  12.8 us
  transfers between devices with their start and end apart: 20, of which 15 were waited for; matrix products, arithmetic and copies ran while one was open for 4% of the time, Pallas kernels for 0%

profile of v1, /device:TPU:32, one launch (start us, length us, event | category | flops | bytes accessed | tf_op | source)
XLA Modules:
  0.0 412.7 jit_solution(5385787165078352291)
XLA Ops:
  12.8 15.3 %all-to-all-start = ((bf16[32,5,768]{2,1,0:T(8,128)(2,1)}), bf16[32,5,768]{2,1,0:T(8,128)(2,1)S(1)}, u32[]{:S(2)}, u32[]{:S(2)}) async-start(bf16[32,5,768]{2,1,0:T(8,128)(2,1)} %bitcast), calls=%async_computation | async-start | bytes 786432 | tf_op jit(solution)/shard_map/all_to_all | solution.py:51
  28.2 26.6 %all-to-all-done = bf16[32,5,768]{2,1,0:T(8,128)(2,1)S(1)} async-done(((bf16[32,5,768]{2,1,0:T(8,128)(2,1)}), bf16[32,5,768]{2,1,0:T(8,128)(2,1)S(1)}, u32[]{:S(2)}, u32[]{:S(2)}) %all-to-all-start) | async-done | bytes 245792 | tf_op jit(solution)/shard_map/all_to_all | solution.py:51
  57.4 3.4 collective-permute-start
  60.8 5.8 %collective-permute-start.1 = (bf16[160,384]{1,0:T(8,128)(2,1)}, bf16[160,384]{1,0:T(8,128)(2,1)}, u32[]{:S(2)}, u32[]{:S(2)}) collective-permute-start(bf16[160,384]{1,0:T(8,128)(2,1)} %get-tuple-element.22), channel_id=1, source_target_pairs={{0,387},{1,0},{2,1},{3,2},{128,3},{129,128},{130,129},{131,130},{2... | collective-permute-start | bytes 368648 | tf_op jit(solution)/shard_map/ppermute | solution.py:18
  69.9 7.8 %collective-permute-start.3 = (bf16[160,384]{1,0:T(8,128)(2,1)}, bf16[160,384]{1,0:T(8,128)(2,1)S(1)}, u32[]{:S(2)}, u32[]{:S(2)}) collective-permute-start(bf16[160,384]{1,0:T(8,128)(2,1)} %collective-permute-done.1), channel_id=1, source_target_pairs={{0,387},{1,0},{2,1},{3,2},{128,3},{129,128},{130,129},{131,130},{2... | collective-permute-start | bytes 368648 | tf_op jit(solution)/shard_map/ppermute | solution.py:18
  79.5 1.9 collective-permute-start.4
  81.5 7.2 %collective-permute-start.5 = (bf16[160,384]{1,0:T(8,128)(2,1)S(1)}, bf16[160,384]{1,0:T(8,128)(2,1)S(1)}, u32[]{:S(2)}, u32[]{:S(2)}) collective-permute-start(bf16[160,384]{1,0:T(8,128)(2,1)S(1)} %collective-permute-done.3), channel_id=1, source_target_pairs={{0,387},{1,0},{2,1},{3,2},{128,3},{129,128},{130,129},{131,130},{2... | collective-permute-start | bytes 368648 | tf_op jit(solution)/shard_map/ppermute | solution.py:18
  89.6 1.9 collective-permute-start.6
  91.6 7.2 %collective-permute-start.7 = (bf16[160,384]{1,0:T(8,128)(2,1)S(1)}, bf16[160,384]{1,0:T(8,128)(2,1)S(1)}, u32[]{:S(2)}, u32[]{:S(2)}) collective-permute-start(bf16[160,384]{1,0:T(8,128)(2,1)S(1)} %collective-permute-done.5), channel_id=1, source_target_pairs={{0,387},{1,0},{2,1},{3,2},{128,3},{129,128},{130,129},{131,130},{2... | collective-permute-start | bytes 368648 | tf_op jit(solution)/shard_map/ppermute | solution.py:18
  99.7 1.9 collective-permute-start.8
  101.7 7.2 %collective-permute-start.9 = (bf16[160,384]{1,0:T(8,128)(2,1)S(1)}, bf16[160,384]{1,0:T(8,128)(2,1)S(1)}, u32[]{:S(2)}, u32[]{:S(2)}) collective-permute-start(bf16[160,384]{1,0:T(8,128)(2,1)S(1)} %collective-permute-done.7), channel_id=1, source_target_pairs={{0,387},{1,0},{2,1},{3,2},{128,3},{129,128},{130,129},{131,130},{2... | collective-permute-start | bytes 368648 | tf_op jit(solution)/shard_map/ppermute | solution.py:18
  110.7 1.9 collective-permute-start.10
  112.8 7.7 %collective-permute-start.11 = (bf16[160,384]{1,0:T(8,128)(2,1)S(1)}, bf16[160,384]{1,0:T(8,128)(2,1)S(1)}, u32[]{:S(2)}, u32[]{:S(2)}) collective-permute-start(bf16[160,384]{1,0:T(8,128)(2,1)S(1)} %collective-permute-done.9), channel_id=1, source_target_pairs={{0,387},{1,0},{2,1},{3,2},{128,3},{129,128},{130,129},{131,130},{2... | collective-permute-start | bytes 368648 | tf_op jit(solution)/shard_map/ppermute | solution.py:18
  120.8 1.9 collective-permute-start.12
  122.9 7.7 %collective-permute-start.13 = (bf16[160,384]{1,0:T(8,128)(2,1)S(1)}, bf16[160,384]{1,0:T(8,128)(2,1)S(1)}, u32[]{:S(2)}, u32[]{:S(2)}) collective-permute-start(bf16[160,384]{1,0:T(8,128)(2,1)S(1)} %collective-permute-done.11), channel_id=1, source_target_pairs={{0,387},{1,0},{2,1},{3,2},{128,3},{129,128},{130,129},{131,130},{2... | collective-permute-start | bytes 368648 | tf_op jit(solution)/shard_map/ppermute | solution.py:18
  133.1 7.9 %collective-permute-done.14 = bf16[160,384]{1,0:T(8,128)(2,1)S(1)} collective-permute-done((bf16[160,384]{1,0:T(8,128)(2,1)S(1)}, bf16[160,384]{1,0:T(8,128)(2,1)S(1)}, u32[]{:S(2)}, u32[]{:S(2)}) %collective-permute-start.14) | collective-permute-done | bytes 122912 | tf_op jit(solution)/shard_map/ppermute | solution.py:15
  143.6 2.7 copy.38
  146.5 2.3 fusion.1
  151.0 2.7 copy.40
  153.8 74.9 %reduce-scatter.7.cloned.1.call-done = bf16[384,160]{1,0:T(8,128)(2,1)} async-done(((bf16[6144,160]{1,0:T(8,128)(2,1)}), bf16[384,160]{1,0:T(8,128)(2,1)}) %reduce-scatter.7.cloned.1.call-update) | async-done | bytes 122896
  229.8 93.6 %reduce-scatter.9.cloned.1.call-done = bf16[384,160]{1,0:T(8,128)(2,1)} async-done(((bf16[6144,160]{1,0:T(8,128)(2,1)}), bf16[384,160]{1,0:T(8,128)(2,1)}) %reduce-scatter.9.cloned.1.call-update) | async-done | bytes 122896
  325.3 12.8 %all-to-all-start.1 = ((bf16[32,5,768]{2,1,0:T(8,128)(2,1)}), bf16[32,5,768]{2,1,0:T(8,128)(2,1)S(1)}, u32[]{:S(2)}, u32[]{:S(2)}) async-start(bf16[32,5,768]{2,1,0:T(8,128)(2,1)} %reshape.67), calls=%async_computation.1 | async-start | bytes 786432 | tf_op jit(solution)/shard_map/all_to_all | solution.py:86
  338.3 26.5 %all-to-all-done.1 = bf16[32,5,768]{2,1,0:T(8,128)(2,1)S(1)} async-done(((bf16[32,5,768]{2,1,0:T(8,128)(2,1)}), bf16[32,5,768]{2,1,0:T(8,128)(2,1)S(1)}, u32[]{:S(2)}, u32[]{:S(2)}) %all-to-all-start.1) | async-done | bytes 245792 | tf_op jit(solution)/shard_map/all_to_all | solution.py:86
  365.4 38.7 %psum.7 = f32[16,2]{1,0:T(8,128)S(1)} all-reduce(f32[16,2]{1,0:T(8,128)S(1)} %reduce_sum.72), channel_id=1, replica_groups=mesh['pipe'=4,'expert'=32,'tensor'=4] {'pipe','tensor'}, use_global_device_ids=true, to_apply=%region_10.11 | all-reduce | flops 32 | bytes 256 | tf_op jit(solution)/shard_map/psum | solution.py:99
  (104 shorter events, 30.2 us)
Async XLA Ops:
  7.2 135.8 %copy-start = (bf16[1,128,6144]{2,1,0:T(8,128)(2,1)S(1)}, bf16[1,128,6144]{2,1,0:T(8,128)(2,1)}, u32[]{:S(2)}) copy-start(bf16[1,128,6144]{2,1,0:T(8,128)(2,1)} %param.12) | copy-start | bytes 4718596
  12.8 42.1 %all-to-all-start = ((bf16[32,5,768]{2,1,0:T(8,128)(2,1)}), bf16[32,5,768]{2,1,0:T(8,128)(2,1)S(1)}, u32[]{:S(2)}, u32[]{:S(2)}) async-start(bf16[32,5,768]{2,1,0:T(8,128)(2,1)} %bitcast), calls=%async_computation | async-start | bytes 786432 | tf_op jit(solution)/shard_map/all_to_all | solution.py:51
  28.1 118.4 %all-gather.2.cloned.1.call-start = ((), (), s32[]{:S(2)}) async-start(), calls=%async_computation.4 | async-start | bytes 2088960 | tf_op jit(solution)/shard_map/all_gather | solution.py:56
  57.3 171.4 %reduce-scatter.7.cloned.1.call-start = ((), (), s32[]{:S(2)}) async-start(), calls=%async_computation.5 | async-start | bytes 3342336
  57.4 10.4 %collective-permute-start = (bf16[160,384]{1,0:T(8,128)(2,1)}, bf16[160,384]{1,0:T(8,128)(2,1)}, u32[]{:S(2)}, u32[]{:S(2)}) collective-permute-start(bf16[160,384]{1,0:T(8,128)(2,1)} %get-tuple-element.22), channel_id=1, source_target_pairs={{0,1},{1,2},{2,3},{3,128},{128,129},{129,130},{130,131},{131,256},... | collective-permute-start | bytes 368648 | tf_op jit(solution)/shard_map/ppermute | solution.py:15
  60.8 9.1 %collective-permute-start.1 = (bf16[160,384]{1,0:T(8,128)(2,1)}, bf16[160,384]{1,0:T(8,128)(2,1)}, u32[]{:S(2)}, u32[]{:S(2)}) collective-permute-start(bf16[160,384]{1,0:T(8,128)(2,1)} %get-tuple-element.22), channel_id=1, source_target_pairs={{0,387},{1,0},{2,1},{3,2},{128,3},{129,128},{130,129},{131,130},{2... | collective-permute-start | bytes 368648 | tf_op jit(solution)/shard_map/ppermute | solution.py:18
  66.8 74.1 %copy-start.3 = (bf16[1,6144,128]{2,1,0:T(8,128)(2,1)S(1)}, bf16[1,6144,128]{2,1,0:T(8,128)(2,1)}, u32[]{:S(2)}) copy-start(bf16[1,6144,128]{2,1,0:T(8,128)(2,1)} %param.11) | copy-start | bytes 4718596
  67.8 11.8 %collective-permute-start.2 = (bf16[160,384]{1,0:T(8,128)(2,1)}, bf16[160,384]{1,0:T(8,128)(2,1)S(1)}, u32[]{:S(2)}, u32[]{:S(2)}) collective-permute-start(bf16[160,384]{1,0:T(8,128)(2,1)} %collective-permute-done), channel_id=1, source_target_pairs={{0,1},{1,2},{2,3},{3,128},{128,129},{129,130},{130,131},{131,256},... | collective-permute-start | bytes 368648 | tf_op jit(solution)/shard_map/ppermute | solution.py:15
  69.9 11.6 %collective-permute-start.3 = (bf16[160,384]{1,0:T(8,128)(2,1)}, bf16[160,384]{1,0:T(8,128)(2,1)S(1)}, u32[]{:S(2)}, u32[]{:S(2)}) collective-permute-start(bf16[160,384]{1,0:T(8,128)(2,1)} %collective-permute-done.1), channel_id=1, source_target_pairs={{0,387},{1,0},{2,1},{3,2},{128,3},{129,128},{130,129},{131,130},{2... | collective-permute-start | bytes 368648 | tf_op jit(solution)/shard_map/ppermute | solution.py:18
  79.5 10.1 %collective-permute-start.4 = (bf16[160,384]{1,0:T(8,128)(2,1)S(1)}, bf16[160,384]{1,0:T(8,128)(2,1)S(1)}, u32[]{:S(2)}, u32[]{:S(2)}) collective-permute-start(bf16[160,384]{1,0:T(8,128)(2,1)S(1)} %collective-permute-done.2), channel_id=1, source_target_pairs={{0,1},{1,2},{2,3},{3,128},{128,129},{129,130},{130,131},{131,256},... | collective-permute-start | bytes 368648 | tf_op jit(solution)/shard_map/ppermute | solution.py:15
  81.5 10.1 %collective-permute-start.5 = (bf16[160,384]{1,0:T(8,128)(2,1)S(1)}, bf16[160,384]{1,0:T(8,128)(2,1)S(1)}, u32[]{:S(2)}, u32[]{:S(2)}) collective-permute-start(bf16[160,384]{1,0:T(8,128)(2,1)S(1)} %collective-permute-done.3), channel_id=1, source_target_pairs={{0,387},{1,0},{2,1},{3,2},{128,3},{129,128},{130,129},{131,130},{2... | collective-permute-start | bytes 368648 | tf_op jit(solution)/shard_map/ppermute | solution.py:18
  89.6 10.1 %collective-permute-start.6 = (bf16[160,384]{1,0:T(8,128)(2,1)S(1)}, bf16[160,384]{1,0:T(8,128)(2,1)S(1)}, u32[]{:S(2)}, u32[]{:S(2)}) collective-permute-start(bf16[160,384]{1,0:T(8,128)(2,1)S(1)} %collective-permute-done.4), channel_id=1, source_target_pairs={{0,1},{1,2},{2,3},{3,128},{128,129},{129,130},{130,131},{131,256},... | collective-permute-start | bytes 368648 | tf_op jit(solution)/shard_map/ppermute | solution.py:15
  91.6 10.1 %collective-permute-start.7 = (bf16[160,384]{1,0:T(8,128)(2,1)S(1)}, bf16[160,384]{1,0:T(8,128)(2,1)S(1)}, u32[]{:S(2)}, u32[]{:S(2)}) collective-permute-start(bf16[160,384]{1,0:T(8,128)(2,1)S(1)} %collective-permute-done.5), channel_id=1, source_target_pairs={{0,387},{1,0},{2,1},{3,2},{128,3},{129,128},{130,129},{131,130},{2... | collective-permute-start | bytes 368648 | tf_op jit(solution)/shard_map/ppermute | solution.py:18
  99.7 10.9 %collective-permute-start.8 = (bf16[160,384]{1,0:T(8,128)(2,1)S(1)}, bf16[160,384]{1,0:T(8,128)(2,1)S(1)}, u32[]{:S(2)}, u32[]{:S(2)}) collective-permute-start(bf16[160,384]{1,0:T(8,128)(2,1)S(1)} %collective-permute-done.6), channel_id=1, source_target_pairs={{0,1},{1,2},{2,3},{3,128},{128,129},{129,130},{130,131},{131,256},... | collective-permute-start | bytes 368648 | tf_op jit(solution)/shard_map/ppermute | solution.py:15
  101.7 11.2 %collective-permute-start.9 = (bf16[160,384]{1,0:T(8,128)(2,1)S(1)}, bf16[160,384]{1,0:T(8,128)(2,1)S(1)}, u32[]{:S(2)}, u32[]{:S(2)}) collective-permute-start(bf16[160,384]{1,0:T(8,128)(2,1)S(1)} %collective-permute-done.7), channel_id=1, source_target_pairs={{0,387},{1,0},{2,1},{3,2},{128,3},{129,128},{130,129},{131,130},{2... | collective-permute-start | bytes 368648 | tf_op jit(solution)/shard_map/ppermute | solution.py:18
  110.7 10.1 %collective-permute-start.10 = (bf16[160,384]{1,0:T(8,128)(2,1)S(1)}, bf16[160,384]{1,0:T(8,128)(2,1)S(1)}, u32[]{:S(2)}, u32[]{:S(2)}) collective-permute-start(bf16[160,384]{1,0:T(8,128)(2,1)S(1)} %collective-permute-done.8), channel_id=1, source_target_pairs={{0,1},{1,2},{2,3},{3,128},{128,129},{129,130},{130,131},{131,256},... | collective-permute-start | bytes 368648 | tf_op jit(solution)/shard_map/ppermute | solution.py:15
  112.8 10.1 %collective-permute-start.11 = (bf16[160,384]{1,0:T(8,128)(2,1)S(1)}, bf16[160,384]{1,0:T(8,128)(2,1)S(1)}, u32[]{:S(2)}, u32[]{:S(2)}) collective-permute-start(bf16[160,384]{1,0:T(8,128)(2,1)S(1)} %collective-permute-done.9), channel_id=1, source_target_pairs={{0,387},{1,0},{2,1},{3,2},{128,3},{129,128},{130,129},{131,130},{2... | collective-permute-start | bytes 368648 | tf_op jit(solution)/shard_map/ppermute | solution.py:18
  120.8 10.1 %collective-permute-start.12 = (bf16[160,384]{1,0:T(8,128)(2,1)S(1)}, bf16[160,384]{1,0:T(8,128)(2,1)S(1)}, u32[]{:S(2)}, u32[]{:S(2)}) collective-permute-start(bf16[160,384]{1,0:T(8,128)(2,1)S(1)} %collective-permute-done.10), channel_id=1, source_target_pairs={{0,1},{1,2},{2,3},{3,128},{128,129},{129,130},{130,131},{131,256},... | collective-permute-start | bytes 368648 | tf_op jit(solution)/shard_map/ppermute | solution.py:15
  122.9 10.1 %collective-permute-start.13 = (bf16[160,384]{1,0:T(8,128)(2,1)S(1)}, bf16[160,384]{1,0:T(8,128)(2,1)S(1)}, u32[]{:S(2)}, u32[]{:S(2)}) collective-permute-start(bf16[160,384]{1,0:T(8,128)(2,1)S(1)} %collective-permute-done.11), channel_id=1, source_target_pairs={{0,387},{1,0},{2,1},{3,2},{128,3},{129,128},{130,129},{131,130},{2... | collective-permute-start | bytes 368648 | tf_op jit(solution)/shard_map/ppermute | solution.py:18
  130.8 10.1 %collective-permute-start.14 = (bf16[160,384]{1,0:T(8,128)(2,1)S(1)}, bf16[160,384]{1,0:T(8,128)(2,1)S(1)}, u32[]{:S(2)}, u32[]{:S(2)}) collective-permute-start(bf16[160,384]{1,0:T(8,128)(2,1)S(1)} %collective-permute-done.12), channel_id=1, source_target_pairs={{0,1},{1,2},{2,3},{3,128},{128,129},{129,130},{130,131},{131,256},... | collective-permute-start | bytes 368648 | tf_op jit(solution)/shard_map/ppermute | solution.py:15
  146.4 176.9 %reduce-scatter.9.cloned.1.call-start = ((), (), s32[]{:S(2)}) async-start(), calls=%async_computation.6 | async-start | bytes 3342336
  153.7 184.4 %copy-start.12 = (f32[16,2]{0,1:T(2,128)S(1)}, f32[16,2]{0,1:T(2,128)}, u32[]{:S(2)}) copy-start(f32[16,2]{0,1:T(2,128)} %param.9) | copy-start | bytes 388
  153.8 184.5 %copy-start.11 = (bf16[16,384]{1,0:T(8,128)(2,1)S(1)}, bf16[16,384]{1,0:T(8,128)(2,1)}, u32[]{:S(2)}) copy-start(bf16[16,384]{1,0:T(8,128)(2,1)} %param.13) | copy-start | bytes 36868
  325.3 39.5 %all-to-all-start.1 = ((bf16[32,5,768]{2,1,0:T(8,128)(2,1)}), bf16[32,5,768]{2,1,0:T(8,128)(2,1)S(1)}, u32[]{:S(2)}, u32[]{:S(2)}) async-start(bf16[32,5,768]{2,1,0:T(8,128)(2,1)} %reshape.67), calls=%async_computation.1 | async-start | bytes 786432 | tf_op jit(solution)/shard_map/all_to_all | solution.py:86
  (9 other events, 21.0 us)
Sparse Core Ops, SparseCore 0:
  57.4 59.3 all-gather.1
  146.5 82.1 reduce-scatter.6
  232.9 90.4 reduce-scatter.8
